TPU v7x, 256 devices: a whole 4x4x8 slice. The times are simulated.
256 devices in a mesh: sec: 16 (over x, y), vel: 16 (over z, core).
Axes of the slice: x: 4, y: 4, z: 8, core: 2. Of those that a mesh axis runs over, the one named last changes fastest.
Arguments:
- distribution: float32 [13824, 4096], P('vel', 'sec'), may hold values from -6 to 6
- collision: float32 [4096], P('sec'), may hold values from 0.05 to 2
- lower_blocks: float32 [25, 4096], P(None, 'sec'), may hold values from -0.6 to 0.6
- upper_blocks: float32 [25, 4096], P(None, 'sec'), may hold values from -0.6 to 0.6
- diag_inverse: float32 [25, 4096], P(None, 'sec'), may hold values from -0.2 to 1.4
Outputs:
- new_distribution: float32 [13824, 4096], P('vel', 'sec')
- macro: float32 [5, 4096], P(None, 'sec')
All inputs are finite; a program needn't handle non-finite values.
Results may differ from a plain program's by a relative error of at most 0.0003.
Values sent between devices are 32-bit elements; how exact they have to be, the bound alone decides.
No kernel may reach another device: no remote copies, remote signals or barrier semaphores. Data moves between devices by JAX's collectives and lax.ppermute only.
A program may use at most 64 MiB of HBM per device.

v0:
```python
import math
import jax
import jax.numpy as jnp
import numpy as np
from jax import lax
from jax.sharding import PartitionSpec as P

NXI = 24
TUBES = 128
JACOBI = 4
NEWTON = 2
HIGH = lax.Precision.HIGHEST
pseudo_rate = 1.0


def passed_along(block, axis, distance):
    devices = range(lax.axis_size(axis))
    route = [(i - distance, i) for i in devices if i - distance in devices]
    return lax.ppermute(block, axis, route)


def extended(array, sides, width):
    for axis, dim in sides:
        count, length = (lax.axis_size(axis), array.shape[dim])
        up = [(i, (i + 1) % count) for i in range(count - 1)]
        down = [(j, i) for i, j in up]
        last = lax.slice_in_dim(array, length - width, length, axis=dim)
        first = lax.slice_in_dim(array, 0, width, axis=dim)
        before = lax.ppermute(last, axis, up)
        after = lax.ppermute(first, axis, down)
        array = jnp.concatenate([before, array, after], axis=dim)
    return array


def hermite_rule(count):
    quarter = math.pi ** (-0.25)
    found = []
    last_slope = 1.0
    for index in range(count // 2):
        if index == 0:
            guess = math.sqrt(2.0 * count + 1.0) - 1.85575 * (2.0 * count + 1.0) ** (-0.16667)
        elif index == 1:
            guess = guess - 1.14 * count**0.426 / guess
        elif index == 2:
            guess = 1.86 * guess - 0.86 * found[0][0]
        elif index == 3:
            guess = 1.91 * guess - 0.91 * found[1][0]
        else:
            guess = 2.0 * guess - found[index - 2][0]
        for repeat in range(60):
            current = quarter
            previous = 0.0
            for order in range(count):
                older = previous
                previous = current
                current = (
                    guess * math.sqrt(2.0 / (order + 1)) * previous
                    - math.sqrt(order / (order + 1.0)) * older
                )
            last_slope = math.sqrt(2.0 * count) * previous
            guess = guess - current / last_slope
        found.append((guess, 2.0 / (last_slope * last_slope)))
    positive = found[::-1]
    points = [-pair[0] for pair in found] + [pair[0] for pair in positive]
    weights = [pair[1] for pair in found] + [pair[1] for pair in positive]
    return (np.array(points), np.array(weights))


def node_tables(axis_points):
    points, weights = hermite_rule(axis_points)
    node_index = np.arange(axis_points**3)
    idx_x = node_index % axis_points
    idx_z = node_index // axis_points % axis_points
    idx_y = node_index // (axis_points * axis_points)
    along_x = points[idx_x]
    along_y = points[idx_y]
    along_z = points[idx_z]
    node_weight = weights[idx_x] * weights[idx_y] * weights[idx_z] / math.pi**1.5
    energy = along_x**2 + along_y**2 + along_z**2 - 1.5
    moment_basis = np.stack([along_x * 0.0 + 1.0, along_x, along_y, along_z, energy])
    norm_scale = np.array([1.0, 0.5, 0.5, 0.5, 1.5])
    return (
        along_x,
        node_weight,
        moment_basis * node_weight[None, :],
        moment_basis / norm_scale[:, None],
    )


def apply_block(matrices, vector):
    shaped = matrices.reshape((5, 5) + vector.shape[1:])
    return jnp.sum(shaped * vector[None], axis=1)


def affine_combine(earlier_map, later_map):
    return (later_map[0] * earlier_map[0], later_map[0] * earlier_map[1] + later_map[1])


def newton_sums(loaded, signed, shift_mass, shift_flow):
    growth = jnp.exp(shift_mass + shift_flow * signed)
    scaled = loaded * growth
    excess = loaded * (growth - 1.0)
    return jnp.stack(
        [
            jnp.sum(scaled),
            jnp.sum(scaled * signed),
            jnp.sum(scaled * signed * signed),
            jnp.sum(excess),
            jnp.sum(excess * signed),
        ]
    )


def newton_update(shift_mass, shift_flow, sums, goal_mass, goal_flow):
    resid_mass = sums[3] - goal_mass
    resid_flow = sums[4] - goal_flow
    determinant = sums[0] * sums[2] - sums[1] * sums[1]
    new_mass = shift_mass - (sums[2] * resid_mass - sums[1] * resid_flow) / determinant
    new_flow = shift_flow - (sums[0] * resid_flow - sums[1] * resid_mass) / determinant
    return (new_mass, new_flow)


def received(block, distance):
    count = lax.axis_size("sec")
    if abs(distance) >= count:
        return jnp.zeros_like(block)
    return passed_along(block, "sec", distance)


def exclusive_inflow(rate, drive, sign):
    count = lax.axis_size("sec")

    def fetch(a, b, distance):
        got = received(jnp.concatenate([a, b], axis=0), sign * distance)
        return (got[:1], got[1:])

    near_a, near_b = fetch(rate, drive, 1)
    span = 1
    if count > 2:
        far_a, far_b = fetch(rate, drive, 2)
        near_a, near_b = (near_a * far_a, near_a * far_b + near_b)
        span = 2
    while span < count - 1:
        got_a, got_b = fetch(near_a, near_b, span)
        near_a, near_b = (near_a * got_a, near_a * got_b + near_b)
        span *= 2
    return near_b


def with_halo(array, width):
    parts = [received(array, d) for d in range(width, 0, -1)]
    parts.append(array)
    parts.extend((received(array, -d) for d in range(1, width + 1)))
    return jnp.concatenate(parts, axis=1)


def body(distribution, collision, lower_blocks, upper_blocks, diag_inverse):
    node_count = distribution.shape[0]
    cell_count = distribution.shape[1]
    length = cell_count // TUBES
    node_rows = node_count // NXI
    half_nodes = NXI // 2
    along_x, node_weight, weighted_np, rebuild_np = node_tables(NXI)
    all_mass = jnp.asarray(node_weight, jnp.float32)
    offset = lax.axis_index("vel") * node_count
    weighted = lax.dynamic_slice_in_dim(
        jnp.asarray(weighted_np, jnp.float32), offset, node_count, 1
    )
    rebuild = lax.dynamic_slice_in_dim(jnp.asarray(rebuild_np, jnp.float32), offset, node_count, 1)
    node_mass = lax.dynamic_slice_in_dim(all_mass, offset, node_count, 0)
    line_signed = jnp.asarray(along_x[:NXI], jnp.float32)
    old_moments = lax.psum(jnp.dot(weighted, distribution, precision=HIGH), "vel")
    target = jnp.dot(rebuild.T, old_moments, precision=HIGH)
    total_length = length * lax.axis_size("sec")
    thickness = collision.reshape(1, 1, length, TUBES)
    node_speed = jnp.abs(line_signed).reshape(1, NXI, 1, 1)
    denominator = node_speed * total_length + thickness + pseudo_rate
    carry_rate = node_speed * total_length / denominator
    drive_term = (
        thickness * target.reshape(node_rows, NXI, length, TUBES)
        + pseudo_rate * distribution.reshape(node_rows, NXI, length, TUBES)
    ) / denominator
    prod_neg, local_neg = lax.associative_scan(
        affine_combine,
        (
            jnp.broadcast_to(carry_rate[:, :half_nodes], (1, half_nodes, length, TUBES)),
            drive_term[:, :half_nodes],
        ),
        reverse=True,
        axis=2,
    )
    prod_pos, local_pos = lax.associative_scan(
        affine_combine,
        (
            jnp.broadcast_to(carry_rate[:, half_nodes:], (1, NXI - half_nodes, length, TUBES)),
            drive_term[:, half_nodes:],
        ),
        axis=2,
    )
    inflow_pos = exclusive_inflow(prod_pos[:, :, -1], local_pos[:, :, -1], 1)
    inflow_neg = exclusive_inflow(prod_neg[:, :, 0], local_neg[:, :, 0], -1)
    field_neg = local_neg + prod_neg * inflow_neg[:, :, None, :]
    field_pos = local_pos + prod_pos * inflow_pos[:, :, None, :]
    half_field = jnp.concatenate([field_neg, field_pos], axis=1).reshape(node_count, cell_count)
    half_moments = lax.psum(jnp.dot(weighted, half_field, precision=HIGH), "vel")
    residual = (half_moments - old_moments).reshape(5, length, TUBES)
    width = min(-(-JACOBI // length), lax.axis_size("sec") - 1)
    blocks = jnp.concatenate([lower_blocks, upper_blocks, diag_inverse], axis=0)
    blocks_wide = with_halo(blocks.reshape(75, length, TUBES), width)
    lower_r = blocks_wide[:25]
    upper_r = blocks_wide[25:50]
    inverse_r = blocks_wide[50:]
    residual_wide = with_halo(residual, width)
    correction = apply_block(inverse_r, residual_wide)
    edge_zero = jnp.zeros((5, 1, TUBES), jnp.float32)
    for sweep_index in range(JACOBI):
        from_left = jnp.concatenate([edge_zero, correction[:, :-1]], axis=1)
        from_right = jnp.concatenate([correction[:, 1:], edge_zero], axis=1)
        correction = apply_block(
            inverse_r,
            residual_wide - apply_block(lower_r, from_left) - apply_block(upper_r, from_right),
        )
    correction = correction[:, width * length : (width + 1) * length].reshape(5, cell_count)
    macro = half_moments + correction
    synthetic = half_field + jnp.dot(rebuild.T, correction, precision=HIGH)
    local_totals = jnp.sum(old_moments - macro, axis=1)[0:2]
    magnitude = jnp.sum(jnp.abs(synthetic), axis=1)
    line_loaded = jnp.sum((node_mass * magnitude).reshape(node_rows, NXI), axis=0)
    first_copy = (lax.axis_index("vel") == 0).astype(jnp.float32)
    gathered = lax.psum(jnp.concatenate([line_loaded, local_totals * first_copy]), ("sec", "vel"))
    loaded = gathered[:NXI]
    goals = gathered[NXI:]
    shift_mass = jnp.zeros((), jnp.float32)
    shift_flow = jnp.zeros((), jnp.float32)
    for newton_turn in range(NEWTON):
        sums = newton_sums(loaded, line_signed, shift_mass, shift_flow)
        shift_mass, shift_flow = newton_update(shift_mass, shift_flow, sums, goals[0], goals[1])
    growth = jnp.exp(shift_mass + shift_flow * line_signed)
    synthetic_rows = synthetic.reshape(node_rows, NXI, cell_count)
    new_distribution = synthetic_rows + jnp.abs(synthetic_rows) * (growth[None, :, None] - 1.0)
    return (new_distribution.reshape(node_count, cell_count), macro)


def solution(mesh):
    in_specs = (P("vel", "sec"), P("sec"), P(None, "sec"), P(None, "sec"), P(None, "sec"))
    out_specs = (P("vel", "sec"), P(None, "sec"))
    return jax.shard_map(body, mesh=mesh, in_specs=in_specs, out_specs=out_specs, check_vma=False)
```

profile of v0, /device:TPU:1, one launch (start us, length us, event | category | flops | bytes accessed | tf_op | source)
XLA Modules:
  0.0 254.2 jit_solution(769121284347335400)
XLA Ops:
  1.5 1.7 reshape.255
  4.5 27.9 %psum.21 = f32[5,256]{1,0:T(8,128)S(1)} all-reduce(f32[5,256]{1,0:T(8,128)S(1)} %fusion.13), channel_id=1, replica_groups=mesh['sec'=16,'vel'=16] {'vel'}, use_global_device_ids=true, to_apply=%region_0.0 | all-reduce | flops 1280 | bytes 10240 | tf_op jit(solution)/shard_map/psum | solution.py:172
  32.4 1.8 fusion.16
  36.0 1.3 collective-permute-start
  37.4 1.3 collective-permute-start.1
  38.8 6.2 %collective-permute-start.10 = (f32[75,2,128]{2,1,0:T(2,128)S(1)}, f32[75,2,128]{2,1,0:T(2,128)S(1)}, u32[]{:S(2)}, u32[]{:S(2)}) collective-permute-start(f32[75,2,128]{2,1,0:T(2,128)S(1)} %reshape.257), channel_id=1, source_target_pairs={{0,32},{16,48},{32,64},{48,80},{64,96},{80,112},{96,128},{112,144}... | collective-permute-start | bytes 230408 | tf_op jit(solution)/shard_map/ppermute | solution.py:19
  45.0 3.2 %collective-permute-start.11 = (f32[75,2,128]{2,1,0:T(2,128)S(1)}, f32[75,2,128]{2,1,0:T(2,128)S(1)}, u32[]{:S(2)}, u32[]{:S(2)}) collective-permute-start(f32[75,2,128]{2,1,0:T(2,128)S(1)} %reshape.257), channel_id=1, source_target_pairs={{0,16},{16,32},{32,48},{48,64},{64,80},{80,96},{96,112},{112,128},... | collective-permute-start | bytes 230408 | tf_op jit(solution)/shard_map/ppermute | solution.py:19
  48.3 1.3 collective-permute-start.12
  52.9 4.7 %collective-permute-start.5 = (f32[37,12,128]{2,0,1:T(8,128)S(1)}, f32[37,12,128]{2,0,1:T(8,128)S(1)}, u32[]{:S(2)}, u32[]{:S(2)}) collective-permute-start(f32[37,12,128]{2,0,1:T(8,128)S(1)} %pad_maximum_fusion.5), channel_id=1, source_target_pairs={{0,16},{16,32},{32,48},{48,64},{64,80},{80,96},{96,112},{112,128},... | collective-permute-start | bytes 681992 | tf_op jit(solution)/shard_map/ppermute | solution.py:19
  57.6 6.8 %collective-permute-start.6 = (f32[37,12,128]{2,0,1:T(8,128)S(1)}, f32[37,12,128]{2,0,1:T(8,128)S(1)}, u32[]{:S(2)}, u32[]{:S(2)}) collective-permute-start(f32[37,12,128]{2,0,1:T(8,128)S(1)} %pad_maximum_fusion.5), channel_id=1, source_target_pairs={{0,32},{16,48},{32,64},{48,80},{64,96},{80,112},{96,128},{112,144}... | collective-permute-start | bytes 681992 | tf_op jit(solution)/shard_map/ppermute | solution.py:19
  64.4 2.1 concatenate.91
  66.7 1.3 collective-permute-start.2
  68.8 5.4 %collective-permute-start.7 = (f32[37,12,128]{2,0,1:T(8,128)S(1)}, f32[37,12,128]{2,0,1:T(8,128)S(1)}, u32[]{:S(2)}, u32[]{:S(2)}) collective-permute-start(f32[37,12,128]{2,0,1:T(8,128)S(1)} %pad_maximum_fusion.6), channel_id=1, source_target_pairs={{0,32},{16,48},{32,64},{48,80},{64,96},{80,112},{96,128},{112,144}... | collective-permute-start | bytes 681992 | tf_op jit(solution)/shard_map/ppermute | solution.py:19
  76.8 4.3 %collective-permute-done.7 = f32[37,12,128]{2,0,1:T(8,128)S(1)} collective-permute-done((f32[37,12,128]{2,0,1:T(8,128)S(1)}, f32[37,12,128]{2,0,1:T(8,128)S(1)}, u32[]{:S(2)}, u32[]{:S(2)}) %collective-permute-start.7) | collective-permute-done | bytes 227360 | tf_op jit(solution)/shard_map/ppermute | solution.py:19
  81.3 8.1 %collective-permute-start.8 = (f32[37,12,128]{2,0,1:T(8,128)S(1)}, f32[37,12,128]{2,0,1:T(8,128)S(1)}, u32[]{:S(2)}, u32[]{:S(2)}) collective-permute-start(f32[37,12,128]{2,0,1:T(8,128)S(1)} %pad_maximum_fusion.7), channel_id=1, source_target_pairs={{0,64},{16,80},{32,96},{48,112},{64,128},{80,144},{96,160},{112,17... | collective-permute-start | bytes 681992 | tf_op jit(solution)/shard_map/ppermute | solution.py:19
  89.4 1.5 collective-permute-done.3
  92.6 5.9 %collective-permute-start.9 = (f32[37,12,128]{2,0,1:T(8,128)S(1)}, f32[37,12,128]{2,0,1:T(8,128)S(1)}, u32[]{:S(2)}, u32[]{:S(2)}) collective-permute-start(f32[37,12,128]{2,0,1:T(8,128)S(1)} %pad_maximum_fusion.8), channel_id=1, source_target_pairs={{0,128},{16,144},{32,160},{48,176},{64,192},{80,208},{96,224},{112... | collective-permute-start | bytes 681992 | tf_op jit(solution)/shard_map/ppermute | solution.py:19
  99.5 2.8 %collective-permute-done.9 = f32[37,12,128]{2,0,1:T(8,128)S(1)} collective-permute-done((f32[37,12,128]{2,0,1:T(8,128)S(1)}, f32[37,12,128]{2,0,1:T(8,128)S(1)}, u32[]{:S(2)}, u32[]{:S(2)}) %collective-permute-start.9) | collective-permute-done | bytes 227360 | tf_op jit(solution)/shard_map/ppermute | solution.py:19
  104.8 36.0 %psum.22 = f32[5,256]{1,0:T(8,128)S(1)} all-reduce(f32[5,256]{1,0:T(8,128)S(1)} %fusion), channel_id=1, replica_groups=mesh['sec'=16,'vel'=16] {'vel'}, use_global_device_ids=true, to_apply=%region_1.0 | all-reduce | flops 1280 | bytes 10240 | tf_op jit(solution)/shard_map/psum | solution.py:205
  140.8 2.7 %collective-permute-start.14 = (f32[5,2,128]{2,1,0:T(2,128)S(1)}, f32[5,2,128]{2,1,0:T(2,128)S(1)}, u32[]{:S(2)}, u32[]{:S(2)}) collective-permute-start(f32[5,2,128]{2,1,0:T(2,128)S(1)} %reshape.259), channel_id=1, source_target_pairs={{0,32},{16,48},{32,64},{48,80},{64,96},{80,112},{96,128},{112,144}... | collective-permute-start | bytes 15368 | tf_op jit(solution)/shard_map/ppermute | solution.py:19
  147.5 1.7 collective-permute-done.16
  149.2 2.9 %collective-permute-done.17 = f32[5,2,128]{2,1,0:T(2,128)S(1)} collective-permute-done((f32[5,2,128]{2,1,0:T(2,128)S(1)}, f32[5,2,128]{2,1,0:T(2,128)S(1)}, u32[]{:S(2)}, u32[]{:S(2)}) %collective-permute-start.17) | collective-permute-done | bytes 5152 | tf_op jit(solution)/shard_map/ppermute | solution.py:19
  152.8 1.9 abs_reduce_fusion
  156.4 79.3 %psum.23 = f32[26]{0:T(128)S(1)} all-reduce(f32[26]{0:T(128)S(1)} %pad_maximum_fusion.10), channel_id=1, replica_groups=mesh['sec'=16,'vel'=16] {'sec','vel'}, use_global_device_ids=true, to_apply=%region_18.0 | all-reduce | flops 26 | bytes 208 | tf_op jit(solution)/shard_map/psum | solution.py:230
  (140 shorter events, 25.1 us)
Async XLA Ops:
  0.6 0.7 copy-start.4
  0.6 0.7 copy-start.6
  1.5 1.7 copy-start
  36.0 2.7 %copy-start.1 = (f32[25,256]{1,0:T(8,128)S(1)}, f32[25,256]{1,0:T(8,128)}, u32[]{:S(2)}) copy-start(f32[25,256]{1,0:T(8,128)} %param.13) | copy-start | bytes 76804
  36.0 2.7 %copy-start.2 = (f32[25,256]{1,0:T(8,128)S(1)}, f32[25,256]{1,0:T(8,128)}, u32[]{:S(2)}) copy-start(f32[25,256]{1,0:T(8,128)} %param.12) | copy-start | bytes 76804
  36.0 2.7 %copy-start.3 = (f32[25,256]{1,0:T(8,128)S(1)}, f32[25,256]{1,0:T(8,128)}, u32[]{:S(2)}) copy-start(f32[25,256]{1,0:T(8,128)} %param.11) | copy-start | bytes 76804
  36.0 30.5 %collective-permute-start = (f32[37,12,128]{2,0,1:T(8,128)S(1)}, f32[37,12,128]{2,0,1:T(8,128)S(1)}, u32[]{:S(2)}, u32[]{:S(2)}) collective-permute-start(f32[37,12,128]{2,0,1:T(8,128)S(1)} %pad_maximum_fusion.1), channel_id=1, source_target_pairs={{16,0},{32,16},{48,32},{64,48},{80,64},{96,80},{112,96},{128,112},... | collective-permute-start | bytes 681992 | tf_op jit(solution)/shard_map/ppermute | solution.py:19
  37.4 29.2 %collective-permute-start.1 = (f32[37,12,128]{2,0,1:T(8,128)S(1)}, f32[37,12,128]{2,0,1:T(8,128)S(1)}, u32[]{:S(2)}, u32[]{:S(2)}) collective-permute-start(f32[37,12,128]{2,0,1:T(8,128)S(1)} %pad_maximum_fusion.1), channel_id=1, source_target_pairs={{32,0},{48,16},{64,32},{80,48},{96,64},{112,80},{128,96},{144,112}... | collective-permute-start | bytes 681992 | tf_op jit(solution)/shard_map/ppermute | solution.py:19
  38.8 12.8 %collective-permute-start.10 = (f32[75,2,128]{2,1,0:T(2,128)S(1)}, f32[75,2,128]{2,1,0:T(2,128)S(1)}, u32[]{:S(2)}, u32[]{:S(2)}) collective-permute-start(f32[75,2,128]{2,1,0:T(2,128)S(1)} %reshape.257), channel_id=1, source_target_pairs={{0,32},{16,48},{32,64},{48,80},{64,96},{80,112},{96,128},{112,144}... | collective-permute-start | bytes 230408 | tf_op jit(solution)/shard_map/ppermute | solution.py:19
  45.0 7.9 %collective-permute-start.11 = (f32[75,2,128]{2,1,0:T(2,128)S(1)}, f32[75,2,128]{2,1,0:T(2,128)S(1)}, u32[]{:S(2)}, u32[]{:S(2)}) collective-permute-start(f32[75,2,128]{2,1,0:T(2,128)S(1)} %reshape.257), channel_id=1, source_target_pairs={{0,16},{16,32},{32,48},{48,64},{64,80},{80,96},{96,112},{112,128},... | collective-permute-start | bytes 230408 | tf_op jit(solution)/shard_map/ppermute | solution.py:19
  48.3 9.4 %collective-permute-start.12 = (f32[75,2,128]{2,1,0:T(2,128)S(1)}, f32[75,2,128]{2,1,0:T(2,128)S(1)}, u32[]{:S(2)}, u32[]{:S(2)}) collective-permute-start(f32[75,2,128]{2,1,0:T(2,128)S(1)} %reshape.257), channel_id=1, source_target_pairs={{16,0},{32,16},{48,32},{64,48},{80,64},{96,80},{112,96},{128,112},... | collective-permute-start | bytes 230408 | tf_op jit(solution)/shard_map/ppermute | solution.py:19
  51.6 12.9 %collective-permute-start.13 = (f32[75,2,128]{2,1,0:T(2,128)S(1)}, f32[75,2,128]{2,1,0:T(2,128)S(1)}, u32[]{:S(2)}, u32[]{:S(2)}) collective-permute-start(f32[75,2,128]{2,1,0:T(2,128)S(1)} %reshape.257), channel_id=1, source_target_pairs={{32,0},{48,16},{64,32},{80,48},{96,64},{112,80},{128,96},{144,112}... | collective-permute-start | bytes 230408 | tf_op jit(solution)/shard_map/ppermute | solution.py:19
  52.9 15.1 %collective-permute-start.5 = (f32[37,12,128]{2,0,1:T(8,128)S(1)}, f32[37,12,128]{2,0,1:T(8,128)S(1)}, u32[]{:S(2)}, u32[]{:S(2)}) collective-permute-start(f32[37,12,128]{2,0,1:T(8,128)S(1)} %pad_maximum_fusion.5), channel_id=1, source_target_pairs={{0,16},{16,32},{32,48},{48,64},{64,80},{80,96},{96,112},{112,128},... | collective-permute-start | bytes 681992 | tf_op jit(solution)/shard_map/ppermute | solution.py:19
  57.6 11.1 %collective-permute-start.6 = (f32[37,12,128]{2,0,1:T(8,128)S(1)}, f32[37,12,128]{2,0,1:T(8,128)S(1)}, u32[]{:S(2)}, u32[]{:S(2)}) collective-permute-start(f32[37,12,128]{2,0,1:T(8,128)S(1)} %pad_maximum_fusion.5), channel_id=1, source_target_pairs={{0,32},{16,48},{32,64},{48,80},{64,96},{80,112},{96,128},{112,144}... | collective-permute-start | bytes 681992 | tf_op jit(solution)/shard_map/ppermute | solution.py:19
  66.7 8.7 %collective-permute-start.2 = (f32[37,12,128]{2,0,1:T(8,128)S(1)}, f32[37,12,128]{2,0,1:T(8,128)S(1)}, u32[]{:S(2)}, u32[]{:S(2)}) collective-permute-start(f32[37,12,128]{2,0,1:T(8,128)S(1)} %pad_maximum_fusion.2), channel_id=1, source_target_pairs={{32,0},{48,16},{64,32},{80,48},{96,64},{112,80},{128,96},{144,112}... | collective-permute-start | bytes 681992 | tf_op jit(solution)/shard_map/ppermute | solution.py:19
  68.8 12.3 %collective-permute-start.7 = (f32[37,12,128]{2,0,1:T(8,128)S(1)}, f32[37,12,128]{2,0,1:T(8,128)S(1)}, u32[]{:S(2)}, u32[]{:S(2)}) collective-permute-start(f32[37,12,128]{2,0,1:T(8,128)S(1)} %pad_maximum_fusion.6), channel_id=1, source_target_pairs={{0,32},{16,48},{32,64},{48,80},{64,96},{80,112},{96,128},{112,144}... | collective-permute-start | bytes 681992 | tf_op jit(solution)/shard_map/ppermute | solution.py:19
  75.5 15.4 %collective-permute-start.3 = (f32[37,12,128]{2,0,1:T(8,128)S(1)}, f32[37,12,128]{2,0,1:T(8,128)S(1)}, u32[]{:S(2)}, u32[]{:S(2)}) collective-permute-start(f32[37,12,128]{2,0,1:T(8,128)S(1)} %pad_maximum_fusion.3), channel_id=1, source_target_pairs={{64,0},{80,16},{96,32},{112,48},{128,64},{144,80},{160,96},{176,11... | collective-permute-start | bytes 681992 | tf_op jit(solution)/shard_map/ppermute | solution.py:19
  81.3 11.2 %collective-permute-start.8 = (f32[37,12,128]{2,0,1:T(8,128)S(1)}, f32[37,12,128]{2,0,1:T(8,128)S(1)}, u32[]{:S(2)}, u32[]{:S(2)}) collective-permute-start(f32[37,12,128]{2,0,1:T(8,128)S(1)} %pad_maximum_fusion.7), channel_id=1, source_target_pairs={{0,64},{16,80},{32,96},{48,112},{64,128},{80,144},{96,160},{112,17... | collective-permute-start | bytes 681992 | tf_op jit(solution)/shard_map/ppermute | solution.py:19
  91.0 8.4 %collective-permute-start.4 = (f32[37,12,128]{2,0,1:T(8,128)S(1)}, f32[37,12,128]{2,0,1:T(8,128)S(1)}, u32[]{:S(2)}, u32[]{:S(2)}) collective-permute-start(f32[37,12,128]{2,0,1:T(8,128)S(1)} %pad_maximum_fusion.4), channel_id=1, source_target_pairs={{128,0},{144,16},{160,32},{176,48},{192,64},{208,80},{224,96},{240... | collective-permute-start | bytes 681992 | tf_op jit(solution)/shard_map/ppermute | solution.py:19
  92.6 9.7 %collective-permute-start.9 = (f32[37,12,128]{2,0,1:T(8,128)S(1)}, f32[37,12,128]{2,0,1:T(8,128)S(1)}, u32[]{:S(2)}, u32[]{:S(2)}) collective-permute-start(f32[37,12,128]{2,0,1:T(8,128)S(1)} %pad_maximum_fusion.8), channel_id=1, source_target_pairs={{0,128},{16,144},{32,160},{48,176},{64,192},{80,208},{96,224},{112... | collective-permute-start | bytes 681992 | tf_op jit(solution)/shard_map/ppermute | solution.py:19
  140.8 6.7 %collective-permute-start.14 = (f32[5,2,128]{2,1,0:T(2,128)S(1)}, f32[5,2,128]{2,1,0:T(2,128)S(1)}, u32[]{:S(2)}, u32[]{:S(2)}) collective-permute-start(f32[5,2,128]{2,1,0:T(2,128)S(1)} %reshape.259), channel_id=1, source_target_pairs={{0,32},{16,48},{32,64},{48,80},{64,96},{80,112},{96,128},{112,144}... | collective-permute-start | bytes 15368 | tf_op jit(solution)/shard_map/ppermute | solution.py:19
  143.6 4.0 %collective-permute-start.15 = (f32[5,2,128]{2,1,0:T(2,128)S(1)}, f32[5,2,128]{2,1,0:T(2,128)S(1)}, u32[]{:S(2)}, u32[]{:S(2)}) collective-permute-start(f32[5,2,128]{2,1,0:T(2,128)S(1)} %reshape.259), channel_id=1, source_target_pairs={{0,16},{16,32},{32,48},{48,64},{64,80},{80,96},{96,112},{112,128},... | collective-permute-start | bytes 15368 | tf_op jit(solution)/shard_map/ppermute | solution.py:19
  144.9 4.4 %collective-permute-start.16 = (f32[5,2,128]{2,1,0:T(2,128)S(1)}, f32[5,2,128]{2,1,0:T(2,128)S(1)}, u32[]{:S(2)}, u32[]{:S(2)}) collective-permute-start(f32[5,2,128]{2,1,0:T(2,128)S(1)} %reshape.259), channel_id=1, source_target_pairs={{16,0},{32,16},{48,32},{64,48},{80,64},{96,80},{112,96},{128,112},... | collective-permute-start | bytes 15368 | tf_op jit(solution)/shard_map/ppermute | solution.py:19
  146.2 6.0 %collective-permute-start.17 = (f32[5,2,128]{2,1,0:T(2,128)S(1)}, f32[5,2,128]{2,1,0:T(2,128)S(1)}, u32[]{:S(2)}, u32[]{:S(2)}) collective-permute-start(f32[5,2,128]{2,1,0:T(2,128)S(1)} %reshape.259), channel_id=1, source_target_pairs={{32,0},{48,16},{64,32},{80,48},{96,64},{112,80},{128,96},{144,112}... | collective-permute-start | bytes 15368 | tf_op jit(solution)/shard_map/ppermute | solution.py:19
  (2 other events, 1.3 us)
where the time goes:
time: 255 us; the launch traced here: 254 us
  blocking collectives  143 us (56%)
  starting transfers between devices  56.1 us (22%)
  between operations  16.8 us (7%)
  waiting for transfers between devices  16.2 us (6%)
  other arithmetic  8.25 us (3%)
  local copies, waits for them, and re-layouts  7.31 us (3%)
  matrix products  6.31 us (2%)
    psum x1, blocking collectives, body(): lax.psum(jnp.concatenate([line_loaded, local_totals * first_copy]), ('sec...  79.3 us
    ppermute x18, starting transfers between devices, passed_along(): return lax.ppermute(block, axis, route)  56.1 us
    psum x1, blocking collectives, body(): lax.psum(jnp.dot(weighted, half_field, precision=HIGH), 'vel')  36 us
    psum x1, blocking collectives, body(): lax.psum(jnp.dot(weighted, distribution, precision=HIGH), 'vel')  27.9 us
    ppermute x18, waiting for transfers between devices, passed_along(): return lax.ppermute(block, axis, route)  16.2 us
  transfers between devices with their start and end apart: 18, of which 9 were waited for; matrix products, arithmetic and copies ran while one was open for 2% of the time, Pallas kernels for 0%

commit v1 on v0

--- a/solution.py
+++ b/solution.py
@@ -227,7 +227,9 @@
     magnitude = jnp.sum(jnp.abs(synthetic), axis=1)
     line_loaded = jnp.sum((node_mass * magnitude).reshape(node_rows, NXI), axis=0)
     first_copy = (lax.axis_index("vel") == 0).astype(jnp.float32)
-    gathered = lax.psum(jnp.concatenate([line_loaded, local_totals * first_copy]), ("sec", "vel"))
+    gathered = lax.psum(
+        lax.psum(jnp.concatenate([line_loaded, local_totals * first_copy]), "vel"), "sec"
+    )
     loaded = gathered[:NXI]
     goals = gathered[NXI:]
     shift_mass = jnp.zeros((), jnp.float32)

time: 255 us -> 238 us (0.933)
  the two profiles are of different devices: /device:TPU:1 before, /device:TPU:4 now
where the time goes in v1:
time: 238 us; the launch traced here: 237 us
  blocking collectives  108 us (45%)
  starting transfers between devices  67 us (28%)
  waiting for transfers between devices  22.6 us (9%)
  between operations  16.8 us (7%)
  other arithmetic  8.25 us (3%)
  local copies, waits for them, and re-layouts  7.31 us (3%)
  matrix products  6.31 us (3%)
    ppermute x18, starting transfers between devices, passed_along(): return lax.ppermute(block, axis, route)  67 us
    psum x1, blocking collectives, body(): lax.psum(lax.psum(jnp.concatenate([line_loaded, local_totals * first_copy...  31.5 us
    psum x1, blocking collectives, body(): lax.psum(jnp.dot(weighted, distribution, precision=HIGH), 'vel')  29.3 us
    psum x1, blocking collectives, body(): lax.psum(jnp.dot(weighted, half_field, precision=HIGH), 'vel')  24.1 us
    psum x1, blocking collectives, body(): lax.psum(jnp.concatenate([line_loaded, local_totals * first_copy]), 'vel')  23.5 us
    ppermute x18, waiting for transfers between devices, passed_along(): return lax.ppermute(block, axis, route)  22.6 us
  transfers between devices with their start and end apart: 18, of which 5 were waited for; matrix products, arithmetic and copies ran while one was open for 2% of the time, Pallas kernels for 0%

profile of v1, /device:TPU:4, one launch (start us, length us, event | category | flops | bytes accessed | tf_op | source)
XLA Modules:
  0.0 236.7 jit_solution(7614940818521832031)
XLA Ops:
  4.5 29.3 %psum.28 = f32[5,256]{1,0:T(8,128)S(1)} all-reduce(f32[5,256]{1,0:T(8,128)S(1)} %fusion.13), channel_id=1, replica_groups=mesh['sec'=16,'vel'=16] {'vel'}, use_global_device_ids=true, to_apply=%region_0.0 | all-reduce | flops 1280 | bytes 10240 | tf_op jit(solution)/shard_map/psum | solution.py:172
  37.5 4.9 %collective-permute-start = (f32[37,12,128]{2,0,1:T(8,128)S(1)}, f32[37,12,128]{2,0,1:T(8,128)S(1)}, u32[]{:S(2)}, u32[]{:S(2)}) collective-permute-start(f32[37,12,128]{2,0,1:T(8,128)S(1)} %pad_maximum_fusion.1), channel_id=1, source_target_pairs={{16,0},{32,16},{48,32},{64,48},{80,64},{96,80},{112,96},{128,112},... | collective-permute-start | bytes 681992 | tf_op jit(solution)/shard_map/ppermute | solution.py:19
  42.4 2.5 %collective-permute-start.1 = (f32[37,12,128]{2,0,1:T(8,128)S(1)}, f32[37,12,128]{2,0,1:T(8,128)S(1)}, u32[]{:S(2)}, u32[]{:S(2)}) collective-permute-start(f32[37,12,128]{2,0,1:T(8,128)S(1)} %pad_maximum_fusion.1), channel_id=1, source_target_pairs={{32,0},{48,16},{64,32},{80,48},{96,64},{112,80},{128,96},{144,112}... | collective-permute-start | bytes 681992 | tf_op jit(solution)/shard_map/ppermute | solution.py:19
  45.0 4.8 %collective-permute-start.10 = (f32[75,2,128]{2,1,0:T(2,128)S(1)}, f32[75,2,128]{2,1,0:T(2,128)S(1)}, u32[]{:S(2)}, u32[]{:S(2)}) collective-permute-start(f32[75,2,128]{2,1,0:T(2,128)S(1)} %reshape.257), channel_id=1, source_target_pairs={{0,32},{16,48},{32,64},{48,80},{64,96},{80,112},{96,128},{112,144}... | collective-permute-start | bytes 230408 | tf_op jit(solution)/shard_map/ppermute | solution.py:19
  51.8 6.0 %collective-permute-start.12 = (f32[75,2,128]{2,1,0:T(2,128)S(1)}, f32[75,2,128]{2,1,0:T(2,128)S(1)}, u32[]{:S(2)}, u32[]{:S(2)}) collective-permute-start(f32[75,2,128]{2,1,0:T(2,128)S(1)} %reshape.257), channel_id=1, source_target_pairs={{16,0},{32,16},{48,32},{64,48},{80,64},{96,80},{112,96},{128,112},... | collective-permute-start | bytes 230408 | tf_op jit(solution)/shard_map/ppermute | solution.py:19
  61.8 2.8 %collective-permute-start.5 = (f32[37,12,128]{2,0,1:T(8,128)S(1)}, f32[37,12,128]{2,0,1:T(8,128)S(1)}, u32[]{:S(2)}, u32[]{:S(2)}) collective-permute-start(f32[37,12,128]{2,0,1:T(8,128)S(1)} %pad_maximum_fusion.5), channel_id=1, source_target_pairs={{0,16},{16,32},{32,48},{48,64},{64,80},{80,96},{96,112},{112,128},... | collective-permute-start | bytes 681992 | tf_op jit(solution)/shard_map/ppermute | solution.py:19
  64.6 4.6 %collective-permute-start.6 = (f32[37,12,128]{2,0,1:T(8,128)S(1)}, f32[37,12,128]{2,0,1:T(8,128)S(1)}, u32[]{:S(2)}, u32[]{:S(2)}) collective-permute-start(f32[37,12,128]{2,0,1:T(8,128)S(1)} %pad_maximum_fusion.5), channel_id=1, source_target_pairs={{0,32},{16,48},{32,64},{48,80},{64,96},{80,112},{96,128},{112,144}... | collective-permute-start | bytes 681992 | tf_op jit(solution)/shard_map/ppermute | solution.py:19
  69.2 2.1 concatenate.91
  71.4 3.7 %collective-permute-start.2 = (f32[37,12,128]{2,0,1:T(8,128)S(1)}, f32[37,12,128]{2,0,1:T(8,128)S(1)}, u32[]{:S(2)}, u32[]{:S(2)}) collective-permute-start(f32[37,12,128]{2,0,1:T(8,128)S(1)} %pad_maximum_fusion.2), channel_id=1, source_target_pairs={{32,0},{48,16},{64,32},{80,48},{96,64},{112,80},{128,96},{144,112}... | collective-permute-start | bytes 681992 | tf_op jit(solution)/shard_map/ppermute | solution.py:19
  76.3 11.3 %collective-permute-start.7 = (f32[37,12,128]{2,0,1:T(8,128)S(1)}, f32[37,12,128]{2,0,1:T(8,128)S(1)}, u32[]{:S(2)}, u32[]{:S(2)}) collective-permute-start(f32[37,12,128]{2,0,1:T(8,128)S(1)} %pad_maximum_fusion.6), channel_id=1, source_target_pairs={{0,32},{16,48},{32,64},{48,80},{64,96},{80,112},{96,128},{112,144}... | collective-permute-start | bytes 681992 | tf_op jit(solution)/shard_map/ppermute | solution.py:19
  87.7 2.4 %collective-permute-start.3 = (f32[37,12,128]{2,0,1:T(8,128)S(1)}, f32[37,12,128]{2,0,1:T(8,128)S(1)}, u32[]{:S(2)}, u32[]{:S(2)}) collective-permute-start(f32[37,12,128]{2,0,1:T(8,128)S(1)} %pad_maximum_fusion.3), channel_id=1, source_target_pairs={{64,0},{80,16},{96,32},{112,48},{128,64},{144,80},{160,96},{176,11... | collective-permute-start | bytes 681992 | tf_op jit(solution)/shard_map/ppermute | solution.py:19
  90.2 4.2 %collective-permute-done.7 = f32[37,12,128]{2,0,1:T(8,128)S(1)} collective-permute-done((f32[37,12,128]{2,0,1:T(8,128)S(1)}, f32[37,12,128]{2,0,1:T(8,128)S(1)}, u32[]{:S(2)}, u32[]{:S(2)}) %collective-permute-start.7) | collective-permute-done | bytes 227360 | tf_op jit(solution)/shard_map/ppermute | solution.py:19
  94.4 3.4 %collective-permute-start.8 = (f32[37,12,128]{2,0,1:T(8,128)S(1)}, f32[37,12,128]{2,0,1:T(8,128)S(1)}, u32[]{:S(2)}, u32[]{:S(2)}) collective-permute-start(f32[37,12,128]{2,0,1:T(8,128)S(1)} %pad_maximum_fusion.7), channel_id=1, source_target_pairs={{0,64},{16,80},{32,96},{48,112},{64,128},{80,144},{96,160},{112,17... | collective-permute-start | bytes 681992 | tf_op jit(solution)/shard_map/ppermute | solution.py:19
  99.3 5.4 %collective-permute-done.8 = f32[37,12,128]{2,0,1:T(8,128)S(1)} collective-permute-done((f32[37,12,128]{2,0,1:T(8,128)S(1)}, f32[37,12,128]{2,0,1:T(8,128)S(1)}, u32[]{:S(2)}, u32[]{:S(2)}) %collective-permute-start.8) | collective-permute-done | bytes 227360 | tf_op jit(solution)/shard_map/ppermute | solution.py:19
  106.2 8.2 %collective-permute-done.9 = f32[37,12,128]{2,0,1:T(8,128)S(1)} collective-permute-done((f32[37,12,128]{2,0,1:T(8,128)S(1)}, f32[37,12,128]{2,0,1:T(8,128)S(1)}, u32[]{:S(2)}, u32[]{:S(2)}) %collective-permute-start.9) | collective-permute-done | bytes 227360 | tf_op jit(solution)/shard_map/ppermute | solution.py:19
  116.9 24.1 %psum.29 = f32[5,256]{1,0:T(8,128)S(1)} all-reduce(f32[5,256]{1,0:T(8,128)S(1)} %fusion), channel_id=1, replica_groups=mesh['sec'=16,'vel'=16] {'vel'}, use_global_device_ids=true, to_apply=%region_1.0 | all-reduce | flops 1280 | bytes 10240 | tf_op jit(solution)/shard_map/psum | solution.py:205
  141.0 3.0 %collective-permute-start.14 = (f32[5,2,128]{2,1,0:T(2,128)S(1)}, f32[5,2,128]{2,1,0:T(2,128)S(1)}, u32[]{:S(2)}, u32[]{:S(2)}) collective-permute-start(f32[5,2,128]{2,1,0:T(2,128)S(1)} %reshape.259), channel_id=1, source_target_pairs={{0,32},{16,48},{32,64},{48,80},{64,96},{80,112},{96,128},{112,144}... | collective-permute-start | bytes 15368 | tf_op jit(solution)/shard_map/ppermute | solution.py:19
  144.0 1.9 collective-permute-start.15
  145.9 6.0 %collective-permute-start.16 = (f32[5,2,128]{2,1,0:T(2,128)S(1)}, f32[5,2,128]{2,1,0:T(2,128)S(1)}, u32[]{:S(2)}, u32[]{:S(2)}) collective-permute-start(f32[5,2,128]{2,1,0:T(2,128)S(1)} %reshape.259), channel_id=1, source_target_pairs={{16,0},{32,16},{48,32},{64,48},{80,64},{96,80},{112,96},{128,112},... | collective-permute-start | bytes 15368 | tf_op jit(solution)/shard_map/ppermute | solution.py:19
  152.0 3.1 %collective-permute-start.17 = (f32[5,2,128]{2,1,0:T(2,128)S(1)}, f32[5,2,128]{2,1,0:T(2,128)S(1)}, u32[]{:S(2)}, u32[]{:S(2)}) collective-permute-start(f32[5,2,128]{2,1,0:T(2,128)S(1)} %reshape.259), channel_id=1, source_target_pairs={{32,0},{48,16},{64,32},{80,48},{96,64},{112,80},{128,96},{144,112}... | collective-permute-start | bytes 15368 | tf_op jit(solution)/shard_map/ppermute | solution.py:19
  155.2 3.8 %collective-permute-done.17 = f32[5,2,128]{2,1,0:T(2,128)S(1)} collective-permute-done((f32[5,2,128]{2,1,0:T(2,128)S(1)}, f32[5,2,128]{2,1,0:T(2,128)S(1)}, u32[]{:S(2)}, u32[]{:S(2)}) %collective-permute-start.17) | collective-permute-done | bytes 5152 | tf_op jit(solution)/shard_map/ppermute | solution.py:19
  159.7 1.9 abs_reduce_fusion
  163.3 23.5 %psum.30 = f32[26]{0:T(128)S(1)} all-reduce(f32[26]{0:T(128)S(1)} %pad_maximum_fusion.10), channel_id=1, replica_groups=mesh['sec'=16,'vel'=16] {'vel'}, use_global_device_ids=true, to_apply=%region_18.0 | all-reduce | flops 26 | bytes 208 | tf_op jit(solution)/shard_map/psum | solution.py:231
  186.8 31.5 %psum.31 = f32[26]{0:T(128)S(1)} all-reduce(f32[26]{0:T(128)S(1)} %psum.30), channel_id=1, replica_groups=mesh['sec'=16,'vel'=16] {'sec'}, use_global_device_ids=true, to_apply=%region_19.0 | all-reduce | flops 26 | bytes 208 | tf_op jit(solution)/shard_map/psum | solution.py:230
  (141 shorter events, 25.4 us)
Async XLA Ops:
  0.6 0.7 copy-start.4
  0.6 0.7 copy-start.6
  1.5 1.7 copy-start
  37.4 7.5 %copy-start.1 = (f32[25,256]{1,0:T(8,128)S(1)}, f32[25,256]{1,0:T(8,128)}, u32[]{:S(2)}) copy-start(f32[25,256]{1,0:T(8,128)} %param.13) | copy-start | bytes 76804
  37.4 7.5 %copy-start.2 = (f32[25,256]{1,0:T(8,128)S(1)}, f32[25,256]{1,0:T(8,128)}, u32[]{:S(2)}) copy-start(f32[25,256]{1,0:T(8,128)} %param.12) | copy-start | bytes 76804
  37.4 7.5 %copy-start.3 = (f32[25,256]{1,0:T(8,128)S(1)}, f32[25,256]{1,0:T(8,128)}, u32[]{:S(2)}) copy-start(f32[25,256]{1,0:T(8,128)} %param.11) | copy-start | bytes 76804
  37.5 33.8 %collective-permute-start = (f32[37,12,128]{2,0,1:T(8,128)S(1)}, f32[37,12,128]{2,0,1:T(8,128)S(1)}, u32[]{:S(2)}, u32[]{:S(2)}) collective-permute-start(f32[37,12,128]{2,0,1:T(8,128)S(1)} %pad_maximum_fusion.1), channel_id=1, source_target_pairs={{16,0},{32,16},{48,32},{64,48},{80,64},{96,80},{112,96},{128,112},... | collective-permute-start | bytes 681992 | tf_op jit(solution)/shard_map/ppermute | solution.py:19
  42.4 28.9 %collective-permute-start.1 = (f32[37,12,128]{2,0,1:T(8,128)S(1)}, f32[37,12,128]{2,0,1:T(8,128)S(1)}, u32[]{:S(2)}, u32[]{:S(2)}) collective-permute-start(f32[37,12,128]{2,0,1:T(8,128)S(1)} %pad_maximum_fusion.1), channel_id=1, source_target_pairs={{32,0},{48,16},{64,32},{80,48},{96,64},{112,80},{128,96},{144,112}... | collective-permute-start | bytes 681992 | tf_op jit(solution)/shard_map/ppermute | solution.py:19
  45.0 14.8 %collective-permute-start.10 = (f32[75,2,128]{2,1,0:T(2,128)S(1)}, f32[75,2,128]{2,1,0:T(2,128)S(1)}, u32[]{:S(2)}, u32[]{:S(2)}) collective-permute-start(f32[75,2,128]{2,1,0:T(2,128)S(1)} %reshape.257), channel_id=1, source_target_pairs={{0,32},{16,48},{32,64},{48,80},{64,96},{80,112},{96,128},{112,144}... | collective-permute-start | bytes 230408 | tf_op jit(solution)/shard_map/ppermute | solution.py:19
  49.9 11.9 %collective-permute-start.11 = (f32[75,2,128]{2,1,0:T(2,128)S(1)}, f32[75,2,128]{2,1,0:T(2,128)S(1)}, u32[]{:S(2)}, u32[]{:S(2)}) collective-permute-start(f32[75,2,128]{2,1,0:T(2,128)S(1)} %reshape.257), channel_id=1, source_target_pairs={{0,16},{16,32},{32,48},{48,64},{64,80},{80,96},{96,112},{112,128},... | collective-permute-start | bytes 230408 | tf_op jit(solution)/shard_map/ppermute | solution.py:19
  51.8 12.8 %collective-permute-start.12 = (f32[75,2,128]{2,1,0:T(2,128)S(1)}, f32[75,2,128]{2,1,0:T(2,128)S(1)}, u32[]{:S(2)}, u32[]{:S(2)}) collective-permute-start(f32[75,2,128]{2,1,0:T(2,128)S(1)} %reshape.257), channel_id=1, source_target_pairs={{16,0},{32,16},{48,32},{64,48},{80,64},{96,80},{112,96},{128,112},... | collective-permute-start | bytes 230408 | tf_op jit(solution)/shard_map/ppermute | solution.py:19
  59.8 9.3 %collective-permute-start.13 = (f32[75,2,128]{2,1,0:T(2,128)S(1)}, f32[75,2,128]{2,1,0:T(2,128)S(1)}, u32[]{:S(2)}, u32[]{:S(2)}) collective-permute-start(f32[75,2,128]{2,1,0:T(2,128)S(1)} %reshape.257), channel_id=1, source_target_pairs={{32,0},{48,16},{64,32},{80,48},{96,64},{112,80},{128,96},{144,112}... | collective-permute-start | bytes 230408 | tf_op jit(solution)/shard_map/ppermute | solution.py:19
  61.8 13.3 %collective-permute-start.5 = (f32[37,12,128]{2,0,1:T(8,128)S(1)}, f32[37,12,128]{2,0,1:T(8,128)S(1)}, u32[]{:S(2)}, u32[]{:S(2)}) collective-permute-start(f32[37,12,128]{2,0,1:T(8,128)S(1)} %pad_maximum_fusion.5), channel_id=1, source_target_pairs={{0,16},{16,32},{32,48},{48,64},{64,80},{80,96},{96,112},{112,128},... | collective-permute-start | bytes 681992 | tf_op jit(solution)/shard_map/ppermute | solution.py:19
  64.6 11.6 %collective-permute-start.6 = (f32[37,12,128]{2,0,1:T(8,128)S(1)}, f32[37,12,128]{2,0,1:T(8,128)S(1)}, u32[]{:S(2)}, u32[]{:S(2)}) collective-permute-start(f32[37,12,128]{2,0,1:T(8,128)S(1)} %pad_maximum_fusion.5), channel_id=1, source_target_pairs={{0,32},{16,48},{32,64},{48,80},{64,96},{80,112},{96,128},{112,144}... | collective-permute-start | bytes 681992 | tf_op jit(solution)/shard_map/ppermute | solution.py:19
  71.4 16.2 %collective-permute-start.2 = (f32[37,12,128]{2,0,1:T(8,128)S(1)}, f32[37,12,128]{2,0,1:T(8,128)S(1)}, u32[]{:S(2)}, u32[]{:S(2)}) collective-permute-start(f32[37,12,128]{2,0,1:T(8,128)S(1)} %pad_maximum_fusion.2), channel_id=1, source_target_pairs={{32,0},{48,16},{64,32},{80,48},{96,64},{112,80},{128,96},{144,112}... | collective-permute-start | bytes 681992 | tf_op jit(solution)/shard_map/ppermute | solution.py:19
  76.3 18.0 %collective-permute-start.7 = (f32[37,12,128]{2,0,1:T(8,128)S(1)}, f32[37,12,128]{2,0,1:T(8,128)S(1)}, u32[]{:S(2)}, u32[]{:S(2)}) collective-permute-start(f32[37,12,128]{2,0,1:T(8,128)S(1)} %pad_maximum_fusion.6), channel_id=1, source_target_pairs={{0,32},{16,48},{32,64},{48,80},{64,96},{80,112},{96,128},{112,144}... | collective-permute-start | bytes 681992 | tf_op jit(solution)/shard_map/ppermute | solution.py:19
  87.7 10.2 %collective-permute-start.3 = (f32[37,12,128]{2,0,1:T(8,128)S(1)}, f32[37,12,128]{2,0,1:T(8,128)S(1)}, u32[]{:S(2)}, u32[]{:S(2)}) collective-permute-start(f32[37,12,128]{2,0,1:T(8,128)S(1)} %pad_maximum_fusion.3), channel_id=1, source_target_pairs={{64,0},{80,16},{96,32},{112,48},{128,64},{144,80},{160,96},{176,11... | collective-permute-start | bytes 681992 | tf_op jit(solution)/shard_map/ppermute | solution.py:19
  94.4 10.2 %collective-permute-start.8 = (f32[37,12,128]{2,0,1:T(8,128)S(1)}, f32[37,12,128]{2,0,1:T(8,128)S(1)}, u32[]{:S(2)}, u32[]{:S(2)}) collective-permute-start(f32[37,12,128]{2,0,1:T(8,128)S(1)} %pad_maximum_fusion.7), channel_id=1, source_target_pairs={{0,64},{16,80},{32,96},{48,112},{64,128},{80,144},{96,160},{112,17... | collective-permute-start | bytes 681992 | tf_op jit(solution)/shard_map/ppermute | solution.py:19
  98.0 8.1 %collective-permute-start.4 = (f32[37,12,128]{2,0,1:T(8,128)S(1)}, f32[37,12,128]{2,0,1:T(8,128)S(1)}, u32[]{:S(2)}, u32[]{:S(2)}) collective-permute-start(f32[37,12,128]{2,0,1:T(8,128)S(1)} %pad_maximum_fusion.4), channel_id=1, source_target_pairs={{128,0},{144,16},{160,32},{176,48},{192,64},{208,80},{224,96},{240... | collective-permute-start | bytes 681992 | tf_op jit(solution)/shard_map/ppermute | solution.py:19
  104.8 9.6 %collective-permute-start.9 = (f32[37,12,128]{2,0,1:T(8,128)S(1)}, f32[37,12,128]{2,0,1:T(8,128)S(1)}, u32[]{:S(2)}, u32[]{:S(2)}) collective-permute-start(f32[37,12,128]{2,0,1:T(8,128)S(1)} %pad_maximum_fusion.8), channel_id=1, source_target_pairs={{0,128},{16,144},{32,160},{48,176},{64,192},{80,208},{96,224},{112... | collective-permute-start | bytes 681992 | tf_op jit(solution)/shard_map/ppermute | solution.py:19
  141.0 14.2 %collective-permute-start.14 = (f32[5,2,128]{2,1,0:T(2,128)S(1)}, f32[5,2,128]{2,1,0:T(2,128)S(1)}, u32[]{:S(2)}, u32[]{:S(2)}) collective-permute-start(f32[5,2,128]{2,1,0:T(2,128)S(1)} %reshape.259), channel_id=1, source_target_pairs={{0,32},{16,48},{32,64},{48,80},{64,96},{80,112},{96,128},{112,144}... | collective-permute-start | bytes 15368 | tf_op jit(solution)/shard_map/ppermute | solution.py:19
  144.0 11.1 %collective-permute-start.15 = (f32[5,2,128]{2,1,0:T(2,128)S(1)}, f32[5,2,128]{2,1,0:T(2,128)S(1)}, u32[]{:S(2)}, u32[]{:S(2)}) collective-permute-start(f32[5,2,128]{2,1,0:T(2,128)S(1)} %reshape.259), channel_id=1, source_target_pairs={{0,16},{16,32},{32,48},{48,64},{64,80},{80,96},{96,112},{112,128},... | collective-permute-start | bytes 15368 | tf_op jit(solution)/shard_map/ppermute | solution.py:19
  145.9 9.2 %collective-permute-start.16 = (f32[5,2,128]{2,1,0:T(2,128)S(1)}, f32[5,2,128]{2,1,0:T(2,128)S(1)}, u32[]{:S(2)}, u32[]{:S(2)}) collective-permute-start(f32[5,2,128]{2,1,0:T(2,128)S(1)} %reshape.259), channel_id=1, source_target_pairs={{16,0},{32,16},{48,32},{64,48},{80,64},{96,80},{112,96},{128,112},... | collective-permute-start | bytes 15368 | tf_op jit(solution)/shard_map/ppermute | solution.py:19
  152.0 7.0 %collective-permute-start.17 = (f32[5,2,128]{2,1,0:T(2,128)S(1)}, f32[5,2,128]{2,1,0:T(2,128)S(1)}, u32[]{:S(2)}, u32[]{:S(2)}) collective-permute-start(f32[5,2,128]{2,1,0:T(2,128)S(1)} %reshape.259), channel_id=1, source_target_pairs={{32,0},{48,16},{64,32},{80,48},{96,64},{112,80},{128,96},{144,112}... | collective-permute-start | bytes 15368 | tf_op jit(solution)/shard_map/ppermute | solution.py:19
  (2 other events, 1.3 us)
